TPU v7x, 32 devices: a whole 2x2x4 slice. The times are simulated.
32 devices in a mesh: grp: 2 (over y), ctx: 2 (over core), tp: 8 (over z, x).
Axes of the slice: x: 2, y: 2, z: 4, core: 2. Of those that a mesh axis runs over, the one named last changes fastest.
Arguments:
- queries: bfloat16 [8192, 8, 192], P(('grp', 'ctx'), 'tp'), parts along dimension 0, may hold values from -70 to 70
- latent_rows: bfloat16 [8192, 576], P(('grp', 'ctx', 'tp')), parts along dimension 0, may hold values from -6 to 6
- doc_ids: int32 [8192], P(('grp', 'ctx', 'tp')), parts along dimension 0, may hold values from 0 to 7, as said below
- key_weight: bfloat16 [512, 1024], P(None, 'tp'), may hold values from -0.25 to 0.25
- value_weight: bfloat16 [512, 1024], P(None, 'tp'), may hold values from -0.25 to 0.25
Outputs:
- attended: bfloat16 [8192, 1024], P(('grp', 'ctx'), 'tp'), parts along dimension 0
There are 2 independent parts, one for each index of `grp`. A program takes and returns all parts, laid end to end along the dimension named above; an argument that names none is the same for every part. Nothing has to cross between parts.
Inputs may be any that keep to these rules, and one draw needn't show every extreme that they name: `doc_ids`: never falling along the tokens.
All inputs are finite; a program needn't handle non-finite values.
Results may differ from a plain program's by a relative error of at most 0.0065.
Values may be sent and summed in bfloat16 or wider, within the bound.
No kernel may reach another device: no remote copies, remote signals or barrier semaphores. Data moves between devices by JAX's collectives and lax.ppermute only.
A program may use at most 64 MiB of HBM per device.

v0:
```python
import math
import jax
import jax.numpy as jnp
from jax import lax
from jax.sharding import PartitionSpec as P

KV_RANK = 512
ROPE_DIM = 64
NOPE_DIM = 128


def passed_along(block, axis, distance):
    devices = range(lax.axis_size(axis))
    route = [(i - distance, i) for i in devices if i - distance in devices]
    return lax.ppermute(block, axis, route)


def project(gathered, key_weight, value_weight):
    count = gathered.shape[0]
    latent_part = gathered[:, :KV_RANK]
    heads_here = key_weight.shape[1] // NOPE_DIM
    value_width = value_weight.shape[1] // heads_here
    key_heads = jnp.dot(latent_part, key_weight, preferred_element_type=jnp.float32).astype(
        jnp.bfloat16
    )
    value_heads = jnp.dot(latent_part, value_weight, preferred_element_type=jnp.float32).astype(
        jnp.bfloat16
    )
    key_heads = jnp.transpose(key_heads.reshape(count, heads_here, NOPE_DIM), (1, 0, 2))
    value_heads = jnp.transpose(value_heads.reshape(count, heads_here, value_width), (1, 0, 2))
    return (key_heads, value_heads, gathered[:, KV_RANK:])


def attend(queries, query_pos, query_docs, key_sets):
    block_rows = queries.shape[0]
    heads_here = queries.shape[1]
    value_width = key_sets[0][1].shape[2]
    tile_rows = min(512, block_rows)
    tile_count = block_rows // tile_rows
    factor = 1.0 / math.sqrt(NOPE_DIM + ROPE_DIM)
    query_heads = jnp.transpose(queries, (1, 0, 2)).reshape(
        heads_here, tile_count, tile_rows, queries.shape[2]
    )
    pos_tiles = query_pos.reshape(tile_count, tile_rows)
    doc_tiles = query_docs.reshape(tile_count, tile_rows)

    def one_head(packed):
        query_one, key_list, value_list = packed

        def one_tile(tile_pack):
            query_tile, tile_pos, tile_docs = tile_pack
            maxima = jnp.full((tile_rows,), -1e30, jnp.float32)
            totals = jnp.zeros((tile_rows,), jnp.float32)
            summed = jnp.zeros((tile_rows, value_width), jnp.float32)
            for number in range(len(key_sets)):
                key_all = key_list[number]
                value_all = value_list[number]
                rope_all = key_sets[number][2]
                docs_all = key_sets[number][3]
                pos_all = key_sets[number][4]
                length = key_all.shape[0]
                key_rows = min(512, length)
                for begin in range(0, length, key_rows):
                    key_tile = key_all[begin : begin + key_rows]
                    rope_tile = rope_all[begin : begin + key_rows]
                    scores = jnp.dot(
                        query_tile[:, :NOPE_DIM], key_tile.T, preferred_element_type=jnp.float32
                    )
                    scores = scores + jnp.dot(
                        query_tile[:, NOPE_DIM:], rope_tile.T, preferred_element_type=jnp.float32
                    )
                    scores = scores * factor
                    visible = (pos_all[None, begin : begin + key_rows] <= tile_pos[:, None]) & (
                        docs_all[None, begin : begin + key_rows] == tile_docs[:, None]
                    )
                    scores = jnp.where(visible, scores, jnp.float32(-1e30))
                    new_maxima = jnp.maximum(maxima, jnp.max(scores, axis=1))
                    rescale = jnp.exp(maxima - new_maxima)
                    weights = jnp.where(
                        visible, jnp.exp(scores - new_maxima[:, None]), jnp.float32(0.0)
                    )
                    totals = totals * rescale + jnp.sum(weights, axis=1)
                    summed = summed * rescale[:, None] + jnp.dot(
                        weights.astype(jnp.bfloat16),
                        value_all[begin : begin + key_rows],
                        preferred_element_type=jnp.float32,
                    )
                    maxima = new_maxima
            return (summed / totals[:, None]).astype(jnp.bfloat16)

        return lax.map(one_tile, (query_one, pos_tiles, doc_tiles))

    key_lists = tuple((entry[0] for entry in key_sets))
    value_lists = tuple((entry[1] for entry in key_sets))
    result = lax.map(one_head, (query_heads, key_lists, value_lists))
    result = result.reshape(heads_here, block_rows, value_width)
    return jnp.transpose(result, (1, 0, 2)).reshape(block_rows, heads_here * value_width)


def body(queries, latent_rows, doc_ids, key_weight, value_weight):
    block_rows = queries.shape[0]
    cycle_size = lax.axis_size("ctx")
    cycle_index = lax.axis_index("ctx")
    offsets = jnp.arange(block_rows, dtype=jnp.int32)
    query_pos = cycle_index * block_rows + offsets
    gathered, own_docs = (
        lax.all_gather(latent_rows, "tp", axis=0, tiled=True),
        lax.all_gather(doc_ids, "tp", axis=0, tiled=True),
    )
    key_heads, value_heads, rope_keys = project(gathered, key_weight, value_weight)
    key_sets = [(key_heads, value_heads, rope_keys, own_docs, query_pos)]
    moving_keys, moving_values, moving_rope, moving_docs = (
        key_heads,
        value_heads,
        rope_keys,
        own_docs,
    )
    moving_keys, moving_values, moving_rope, moving_docs = passed_along(
        (moving_keys, moving_values, moving_rope, moving_docs), "ctx", 1
    )
    source = (cycle_index - 1) % cycle_size
    key_sets.append(
        (moving_keys, moving_values, moving_rope, moving_docs, source * block_rows + offsets)
    )
    return attend(queries, query_pos, own_docs, key_sets)


def solution(mesh):
    placed = (
        P(("grp", "ctx"), "tp", None),
        P(("grp", "ctx", "tp"), None),
        P(("grp", "ctx", "tp")),
        P(None, "tp"),
        P(None, "tp"),
    )
    return jax.shard_map(
        body, mesh=mesh, in_specs=placed, out_specs=P(("grp", "ctx"), "tp"), check_vma=False
    )
```

profile of v0, /device:TPU:0, one launch (start us, length us, event | category | flops | bytes accessed | tf_op | source)
XLA Modules:
  0.0 189.9 jit_solution(10066499171351850689)
XLA Ops:
  6.5 1.9 %copy.9 = bf16[256,576]{1,0:T(8,128)(2,1)} copy(bf16[256,576]{0,1:T(8,128)(2,1)} %param.8) | data formatting | bytes 589824 | tf_op args[1]
  8.5 58.5 %all-gather.3.cloned.1.call-done = bf16[2048,576]{1,0:T(8,128)(2,1)} async-done(((bf16[256,576]{1,0:T(8,128)(2,1)}), bf16[2048,576]{1,0:T(8,128)(2,1)}) %all-gather.3.cloned.1.call-update) | async-done | bytes 2359312 | tf_op jit(solution)/shard_map/all_gather | solution.py:107
  66.9 3.3 %convolution_convert_fusion = bf16[2048,128]{1,0:T(8,128)(2,1)} fusion(bf16[512,128]{1,0:T(8,128)(2,1)S(1)} %copy-done, bf16[2048,576]{1,0:T(8,128)(2,1)} %all-gather.3.cloned.1.call-done), kind=kOutput, calls=%fused_computation.193 | convolution fusion | flops 268697600 | bytes 2752512 | tf_op jit(solution)/shard_map/dot_general | solution.py:26
  70.2 2.2 %collective-permute-start.3 = (bf16[1,2048,128]{2,1,0:T(8,128)(2,1)}, bf16[1,2048,128]{2,1,0:T(8,128)(2,1)}, u32[]{:S(2)}, u32[]{:S(2)}) collective-permute-start(bf16[1,2048,128]{2,1,0:T(8,128)(2,1)} %bitcast.9), channel_id=1, source_target_pairs={{0,8},{1,9},{2,10},{3,11},{4,12},{5,13},{6,14},{7,15},{16,24},{17,... | collective-permute-start | bytes 1572872 | tf_op jit(solution)/shard_map/ppermute | solution.py:15
  72.4 0.7 convolution_convert_fusion.1
  73.1 1.3 collective-permute-start.1
  74.5 1.3 collective-permute-start.2
  75.8 18.6 %all-gather = s32[8,1,256]{2,1,0:T(1,128)S(1)} all-gather(s32[1,1,256]{2,1,0:T(1,128)S(1)} %bitcast.67), channel_id=1, replica_groups=mesh['grp'=2,'ctx'=2,'tp'=8] {'tp'}, dimensions={0}, use_global_device_ids=true | all-gather | bytes 9216 | tf_op jit(solution)/shard_map/all_gather | solution.py:108
  94.4 1.3 collective-permute-start
  95.8 1.4 copy.8
  97.3 85.8 %while.17 = (s32[]{:T(128)}, bf16[4,512,128]{2,1,0:T(8,128)(2,1)}, s32[2048]{0:T(1024)S(1)}, s32[4,512]{1,0:T(4,128)S(1)}, s32[2048]{0:T(1024)S(1)}, /*index=5*/...) while((s32[]{:T(128)}, bf16[4,512,128]{2,1,0:T(8,128)(2,1)}, ...), condition=%wide.region_17.18_spmd, body=%wide.region_0.17_spmd.sunk | while | flops 1383147008 | bytes 51794588 | solution.py:91
  99.9 0.4 fusion.278
  102.8 0.4 fusion.269
  103.3 1.5 fusion.287
  104.8 1.5 fusion.286
  106.4 1.4 fusion.288
  107.8 1.5 fusion.289
  109.3 1.5 fusion.290
  110.8 1.5 fusion.291
  112.2 1.5 fusion.292
  113.7 1.5 fusion.293
  115.1 1.5 fusion.294
  116.6 2.2 %fusion.295 = bf16[4,512,128]{2,1,0:T(8,128)(2,1)} fusion(bf16[4,512,128]{2,1,0:T(8,128)(2,1)} %get-tuple-element.453, s32[]{:T(128)} %get-tuple-element.452, f32[512,128]{1,0:T(8,128)S(1)} %fusion.294, f32[512,512]{0,1:T(8,128)S(1)} %get-tuple-element.411, f32[512]{0:T(512)S(1)} %get-tuple-element.412, s32[512]{0:T(512)S(1)} %bitcast.45, ...), kind=kOutput, calls=%fused_computation.42.clone.1 | convolution fusion | flops 68878336 | bytes 1585664 | tf_op jit(solution)/shard_map/while/body/eval_jaxpr/while/body/eval_jaxpr/dot_general | solution.py:83
  119.8 0.4 fusion.274
  120.6 0.4 fusion.276
  121.3 0.4 fusion.278
  122.8 0.4 fusion.282
  124.3 0.4 fusion.269
  124.7 1.5 fusion.287
  126.3 1.5 fusion.286
  127.8 1.4 fusion.288
  129.3 1.5 fusion.289
  130.7 1.5 fusion.290
  132.2 1.5 fusion.291
  133.7 1.5 fusion.292
  135.1 1.5 fusion.293
  136.6 1.5 fusion.294
  138.0 2.2 %fusion.295 = bf16[4,512,128]{2,1,0:T(8,128)(2,1)} fusion(bf16[4,512,128]{2,1,0:T(8,128)(2,1)} %get-tuple-element.453, s32[]{:T(128)} %get-tuple-element.452, f32[512,128]{1,0:T(8,128)S(1)} %fusion.294, f32[512,512]{0,1:T(8,128)S(1)} %get-tuple-element.411, f32[512]{0:T(512)S(1)} %get-tuple-element.412, s32[512]{0:T(512)S(1)} %bitcast.45, ...), kind=kOutput, calls=%fused_computation.42.clone.1 | convolution fusion | flops 68878336 | bytes 1585664 | tf_op jit(solution)/shard_map/while/body/eval_jaxpr/while/body/eval_jaxpr/dot_general | solution.py:83
  141.3 0.4 fusion.274
  142.0 0.4 fusion.276
  142.8 0.4 fusion.278
  145.7 0.4 fusion.269
  146.2 1.5 fusion.287
  147.7 1.5 fusion.286
  149.3 1.4 fusion.288
  150.7 1.5 fusion.289
  152.2 1.5 fusion.290
  153.7 1.5 fusion.291
  155.1 1.5 fusion.292
  156.6 1.5 fusion.293
  158.0 1.5 fusion.294
  159.5 2.2 %fusion.295 = bf16[4,512,128]{2,1,0:T(8,128)(2,1)} fusion(bf16[4,512,128]{2,1,0:T(8,128)(2,1)} %get-tuple-element.453, s32[]{:T(128)} %get-tuple-element.452, f32[512,128]{1,0:T(8,128)S(1)} %fusion.294, f32[512,512]{0,1:T(8,128)S(1)} %get-tuple-element.411, f32[512]{0:T(512)S(1)} %get-tuple-element.412, s32[512]{0:T(512)S(1)} %bitcast.45, ...), kind=kOutput, calls=%fused_computation.42.clone.1 | convolution fusion | flops 68878336 | bytes 1585664 | tf_op jit(solution)/shard_map/while/body/eval_jaxpr/while/body/eval_jaxpr/dot_general | solution.py:83
  163.5 0.4 fusion.276
  167.2 0.4 fusion.269
  167.6 1.5 fusion.287
  169.2 1.5 fusion.286
  170.7 1.4 fusion.288
  172.2 1.5 fusion.289
  173.6 1.5 fusion.290
  175.1 1.5 fusion.291
  176.6 1.5 fusion.292
  178.0 1.5 fusion.293
  179.5 1.5 fusion.294
  180.9 2.2 %fusion.295 = bf16[4,512,128]{2,1,0:T(8,128)(2,1)} fusion(bf16[4,512,128]{2,1,0:T(8,128)(2,1)} %get-tuple-element.453, s32[]{:T(128)} %get-tuple-element.452, f32[512,128]{1,0:T(8,128)S(1)} %fusion.294, f32[512,512]{0,1:T(8,128)S(1)} %get-tuple-element.411, f32[512]{0:T(512)S(1)} %get-tuple-element.412, s32[512]{0:T(512)S(1)} %bitcast.45, ...), kind=kOutput, calls=%fused_computation.42.clone.1 | convolution fusion | flops 68878336 | bytes 1585664 | tf_op jit(solution)/shard_map/while/body/eval_jaxpr/while/body/eval_jaxpr/dot_general | solution.py:83
  (95 shorter events, 18.2 us)
Async XLA Ops:
  6.5 60.4 %copy-start = (bf16[512,128]{1,0:T(8,128)(2,1)S(1)}, bf16[512,128]{1,0:T(8,128)(2,1)}, u32[]{:S(2)}) copy-start(bf16[512,128]{1,0:T(8,128)(2,1)} %param.11) | copy-start | bytes 393220
  6.5 65.9 %copy-start.3 = (bf16[512,128]{1,0:T(8,128)(2,1)S(1)}, bf16[512,128]{1,0:T(8,128)(2,1)}, u32[]{:S(2)}) copy-start(bf16[512,128]{1,0:T(8,128)(2,1)} %param.10) | copy-start | bytes 393220
  6.5 60.4 %all-gather.3.cloned.1.call-start = ((), (), s32[]{:S(2)}) async-start(), calls=%async_computation | async-start | bytes 2949120 | tf_op jit(solution)/shard_map/all_gather | solution.py:107
  66.9 5.5 %copy-start.1 = (bf16[2048,576]{1,0:T(8,128)(2,1)S(1)}, bf16[2048,576]{1,0:T(8,128)(2,1)}, u32[]{:S(2)}) copy-start(bf16[2048,576]{1,0:T(8,128)(2,1)} %all-gather.3.cloned.1.call-done) | copy-start | bytes 7077892
  70.2 5.6 %copy-start.2 = (s32[256]{0:T(256)S(1)}, s32[256]{0:T(256)}, u32[]{:S(2)}) copy-start(s32[256]{0:T(256)} %param.9) | copy-start | bytes 3076
  70.2 27.1 %collective-permute-start.3 = (bf16[1,2048,128]{2,1,0:T(8,128)(2,1)}, bf16[1,2048,128]{2,1,0:T(8,128)(2,1)}, u32[]{:S(2)}, u32[]{:S(2)}) collective-permute-start(bf16[1,2048,128]{2,1,0:T(8,128)(2,1)} %bitcast.9), channel_id=1, source_target_pairs={{0,8},{1,9},{2,10},{3,11},{4,12},{5,13},{6,14},{7,15},{16,24},{17,... | collective-permute-start | bytes 1572872 | tf_op jit(solution)/shard_map/ppermute | solution.py:15
  73.1 24.2 %collective-permute-start.1 = (bf16[1,2048,128]{2,1,0:T(8,128)(2,1)S(1)}, bf16[1,2048,128]{2,1,0:T(8,128)(2,1)S(1)}, u32[]{:S(2)}, u32[]{:S(2)}) collective-permute-start(bf16[1,2048,128]{2,1,0:T(8,128)(2,1)S(1)} %bitcast.26), channel_id=1, source_target_pairs={{0,8},{1,9},{2,10},{3,11},{4,12},{5,13},{6,14},{7,15},{16,24},{17,... | collective-permute-start | bytes 1572872 | tf_op jit(solution)/shard_map/ppermute | solution.py:15
  74.5 22.8 %collective-permute-start.2 = (bf16[2048,64]{1,0:T(8,128)(2,1)S(1)}, bf16[2048,64]{1,0:T(8,128)(2,1)S(1)}, u32[]{:S(2)}, u32[]{:S(2)}) collective-permute-start(bf16[2048,64]{1,0:T(8,128)(2,1)S(1)} %slice.151), channel_id=1, source_target_pairs={{0,8},{1,9},{2,10},{3,11},{4,12},{5,13},{6,14},{7,15},{16,24},{17,... | collective-permute-start | bytes 786440 | tf_op jit(solution)/shard_map/ppermute | solution.py:15
  94.4 2.8 %collective-permute-start = (s32[2048]{0:T(1024)S(1)}, s32[2048]{0:T(1024)S(1)}, u32[]{:S(2)}, u32[]{:S(2)}) collective-permute-start(s32[2048]{0:T(1024)S(1)} %bitcast.65), channel_id=1, source_target_pairs={{0,8},{1,9},{2,10},{3,11},{4,12},{5,13},{6,14},{7,15},{16,24},{17,... | collective-permute-start | bytes 24584 | tf_op jit(solution)/shard_map/ppermute | solution.py:15
Sparse Core Ops, SparseCore 0:
  9.5 57.3 all-gather.2
where the time goes:
time: 191 us; the launch traced here: 190 us
  matrix products  76.6 us (40%)
  waiting for transfers between devices  58.5 us (31%)
  blocking collectives  18.6 us (10%)
  between operations  13.5 us (7%)
  other arithmetic  12.4 us (6%)
  starting transfers between devices  6.13 us (3%)
  local copies, waits for them, and re-layouts  3.58 us (2%)
    all_gather x1, waiting for transfers between devices, body(): lax.all_gather(latent_rows, 'tp', axis=0, tiled=True)  58.5 us
    dot_general x32, matrix products, one_tile(): jnp.dot(weights.astype(jnp.bfloat16), value_all[begin:begin + key_rows],...  49.3 us
    all_gather x1, blocking collectives, body(): lax.all_gather(doc_ids, 'tp', axis=0, tiled=True)  18.6 us
    dot_general x32, matrix products, one_tile(): jnp.dot(query_tile[:, NOPE_DIM:], rope_tile.T, preferred_element_type=jnp...  13.9 us
    reduce_sum x8, other arithmetic, one_tile(): totals = totals * rescale + jnp.sum(weights, axis=1)  12.2 us
    dot_general x32, matrix products, one_tile(): jnp.dot(query_tile[:, :NOPE_DIM], key_tile.T, preferred_element_type=jnp....  9.49 us
    ppermute x4, starting transfers between devices, passed_along(): return lax.ppermute(block, axis, route)  6.13 us
  transfers between devices with their start and end apart: 5, of which 1 were waited for; matrix products, arithmetic and copies ran while one was open for 1% of the time, Pallas kernels for 0%

commit v1 on v0

--- a/solution.py
+++ b/solution.py
@@ -7,6 +7,28 @@
 KV_RANK = 512
 ROPE_DIM = 64
 NOPE_DIM = 128
+
+
+def joined_along(blocks, dim):
+    blocks = jnp.moveaxis(blocks, 0, dim)
+    shape = blocks.shape
+    return blocks.reshape(*shape[:dim], shape[dim] * shape[dim + 1], *shape[dim + 2 :])
+
+
+def collect(x, axis, dim):
+    length = lax.axis_size(axis)
+    pairs = [(i, (i + 1) % length) for i in range(length)]
+    back = [(b, a) for a, b in pairs]
+    lower, upper = ([], [])
+    for lap in range(length - 1):
+        if lap % 2 == 0:
+            lower.append(lax.ppermute(lower[-1] if lower else x, axis, pairs))
+        else:
+            upper.append(lax.ppermute(upper[-1] if upper else x, axis, back))
+    tiles = jnp.stack([*lower[::-1], x, *upper])
+    shift = lax.axis_index(axis) - len(lower)
+    tiles = tiles[(jnp.arange(length) - shift) % length]
+    return joined_along(tiles, dim)
 
 
 def passed_along(block, axis, distance):
@@ -104,7 +126,7 @@
     offsets = jnp.arange(block_rows, dtype=jnp.int32)
     query_pos = cycle_index * block_rows + offsets
     gathered, own_docs = (
-        lax.all_gather(latent_rows, "tp", axis=0, tiled=True),
+        collect(latent_rows, "tp", 0),
         lax.all_gather(doc_ids, "tp", axis=0, tiled=True),
     )
     key_heads, value_heads, rope_keys = project(gathered, key_weight, value_weight)

time: 191 us -> 182 us (0.953)
  waiting for transfers between devices: 58.5 us -> 25 us
  starting transfers between devices: 6.13 us -> 34.8 us
  between operations: 13.5 us -> 0.19 us
  local copies, waits for them, and re-layouts: 3.58 us -> 12.5 us
    all_gather x1 -> x0, waiting for transfers between devices: 58.5 us -> none  [body(): lax.all_gather(latent_rows, 'tp', axis=0, tiled=True)]
    ppermute x0 -> x7, starting transfers between devices: none -> 28.6 us  [the longest x3 20.7 us: collect(): upper.append(lax.ppermute(upper[-1] if upper else x, axis, back))]
    ppermute x0 -> x7, waiting for transfers between devices: none -> 24.9 us  [the longest x4 24.9 us: collect(): lower.append(lax.ppermute(lower[-1] if lower else x, axis, pairs))]
    gather x0 -> x2, local copies, waits for them, and re-layouts: none -> 4.94 us  [collect(): tiles = tiles[(jnp.arange(length) - shift) % length]]
    unnamed x10 -> x18, local copies, waits for them, and re-layouts: 3.35 us -> 6.57 us
  transfers between devices with their start and end apart: 5 -> 11, of which waited for: 1 -> 4; matrix products, arithmetic and copies ran while one was open for 1% -> 4% of each run, Pallas kernels for 0% -> 0%
where the time goes in v1:
time: 182 us; the launch traced here: 181 us
  matrix products  76.9 us (42%)
  starting transfers between devices  34.8 us (19%)
  waiting for transfers between devices  25 us (14%)
  blocking collectives  18.9 us (10%)
  local copies, waits for them, and re-layouts  12.5 us (7%)
  other arithmetic  12.5 us (7%)
    dot_general x32, matrix products, one_tile(): jnp.dot(weights.astype(jnp.bfloat16), value_all[begin:begin + key_rows],...  49.5 us
    ppermute x4, waiting for transfers between devices, collect(): lower.append(lax.ppermute(lower[-1] if lower else x, axis, pairs))  24.9 us
    ppermute x3, starting transfers between devices, collect(): upper.append(lax.ppermute(upper[-1] if upper else x, axis, back))  20.7 us
    all_gather x1, blocking collectives, body(): lax.all_gather(doc_ids, 'tp', axis=0, tiled=True)  18.9 us
    dot_general x32, matrix products, one_tile(): jnp.dot(query_tile[:, NOPE_DIM:], rope_tile.T, preferred_element_type=jnp...  14 us
    reduce_sum x8, other arithmetic, one_tile(): totals = totals * rescale + jnp.sum(weights, axis=1)  12.2 us
    dot_general x32, matrix products, one_tile(): jnp.dot(query_tile[:, :NOPE_DIM], key_tile.T, preferred_element_type=jnp....  9.51 us
    ppermute x4, starting transfers between devices, collect(): lower.append(lax.ppermute(lower[-1] if lower else x, axis, pairs))  7.9 us
  transfers between devices with their start and end apart: 11, of which 4 were waited for; matrix products, arithmetic and copies ran while one was open for 4% of the time, Pallas kernels for 0%

profile of v1, /device:TPU:0, one launch (start us, length us, event | category | flops | bytes accessed | tf_op | source)
XLA Modules:
  0.0 181.3 jit_solution(18239230896418566835)
XLA Ops:
  0.0 2.9 %collective-permute-start = (bf16[256,576]{0,1:T(8,128)(2,1)}, bf16[256,576]{0,1:T(8,128)(2,1)S(1)}, u32[]{:S(2)}, u32[]{:S(2)}) collective-permute-start(bf16[256,576]{0,1:T(8,128)(2,1)} %param.8), channel_id=1, source_target_pairs={{0,1},{1,2},{2,3},{3,4},{4,5},{5,6},{6,7},{7,0},{8,9},{9,10},{10,1... | collective-permute-start | bytes 884744 | tf_op jit(solution)/shard_map/ppermute | solution.py:25
  2.9 10.3 %collective-permute-done = bf16[256,576]{0,1:T(8,128)(2,1)S(1)} collective-permute-done((bf16[256,576]{0,1:T(8,128)(2,1)}, bf16[256,576]{0,1:T(8,128)(2,1)S(1)}, u32[]{:S(2)}, u32[]{:S(2)}) %collective-permute-start) | collective-permute-done | bytes 294944 | tf_op jit(solution)/shard_map/ppermute | solution.py:25
  13.2 4.7 %collective-permute-start.4 = (bf16[256,576]{0,1:T(8,128)(2,1)}, bf16[256,576]{0,1:T(8,128)(2,1)S(1)}, u32[]{:S(2)}, u32[]{:S(2)}) collective-permute-start(bf16[256,576]{0,1:T(8,128)(2,1)} %param.8), channel_id=1, source_target_pairs={{1,0},{2,1},{3,2},{4,3},{5,4},{6,5},{7,6},{0,7},{9,8},{10,9},{11,1... | collective-permute-start | bytes 884744 | tf_op jit(solution)/shard_map/ppermute | solution.py:27
  18.0 7.6 %collective-permute-done.1 = bf16[256,576]{0,1:T(8,128)(2,1)S(1)} collective-permute-done((bf16[256,576]{0,1:T(8,128)(2,1)S(1)}, bf16[256,576]{0,1:T(8,128)(2,1)S(1)}, u32[]{:S(2)}, u32[]{:S(2)}) %collective-permute-start.1) | collective-permute-done | bytes 294944 | tf_op jit(solution)/shard_map/ppermute | solution.py:25
  25.5 2.5 %collective-permute-start.2 = (bf16[256,576]{0,1:T(8,128)(2,1)S(1)}, bf16[256,576]{0,1:T(8,128)(2,1)S(1)}, u32[]{:S(2)}, u32[]{:S(2)}) collective-permute-start(bf16[256,576]{0,1:T(8,128)(2,1)S(1)} %collective-permute-done.1), channel_id=1, source_target_pairs={{0,1},{1,2},{2,3},{3,4},{4,5},{5,6},{6,7},{7,0},{8,9},{9,10},{10,1... | collective-permute-start | bytes 884744 | tf_op jit(solution)/shard_map/ppermute | solution.py:25
  28.0 7.4 %collective-permute-start.5 = (bf16[256,576]{0,1:T(8,128)(2,1)S(1)}, bf16[256,576]{0,1:T(8,128)(2,1)S(1)}, u32[]{:S(2)}, u32[]{:S(2)}) collective-permute-start(bf16[256,576]{0,1:T(8,128)(2,1)S(1)} %collective-permute-done.4), channel_id=1, source_target_pairs={{1,0},{2,1},{3,2},{4,3},{5,4},{6,5},{7,6},{0,7},{9,8},{10,9},{11,1... | collective-permute-start | bytes 884744 | tf_op jit(solution)/shard_map/ppermute | solution.py:27
  35.4 4.0 %collective-permute-done.2 = bf16[256,576]{0,1:T(8,128)(2,1)S(1)} collective-permute-done((bf16[256,576]{0,1:T(8,128)(2,1)S(1)}, bf16[256,576]{0,1:T(8,128)(2,1)S(1)}, u32[]{:S(2)}, u32[]{:S(2)}) %collective-permute-start.2) | collective-permute-done | bytes 294944 | tf_op jit(solution)/shard_map/ppermute | solution.py:25
  39.4 2.5 %collective-permute-start.3 = (bf16[256,576]{0,1:T(8,128)(2,1)S(1)}, bf16[256,576]{0,1:T(8,128)(2,1)S(1)}, u32[]{:S(2)}, u32[]{:S(2)}) collective-permute-start(bf16[256,576]{0,1:T(8,128)(2,1)S(1)} %collective-permute-done.2), channel_id=1, source_target_pairs={{0,1},{1,2},{2,3},{3,4},{4,5},{5,6},{6,7},{7,0},{8,9},{9,10},{10,1... | collective-permute-start | bytes 884744 | tf_op jit(solution)/shard_map/ppermute | solution.py:25
  42.0 8.6 %collective-permute-start.6 = (bf16[256,576]{0,1:T(8,128)(2,1)S(1)}, bf16[256,576]{0,1:T(8,128)(2,1)S(1)}, u32[]{:S(2)}, u32[]{:S(2)}) collective-permute-start(bf16[256,576]{0,1:T(8,128)(2,1)S(1)} %collective-permute-done.5), channel_id=1, source_target_pairs={{1,0},{2,1},{3,2},{4,3},{5,4},{6,5},{7,6},{0,7},{9,8},{10,9},{11,1... | collective-permute-start | bytes 884744 | tf_op jit(solution)/shard_map/ppermute | solution.py:27
  50.6 3.0 %collective-permute-done.3 = bf16[256,576]{0,1:T(8,128)(2,1)S(1)} collective-permute-done((bf16[256,576]{0,1:T(8,128)(2,1)S(1)}, bf16[256,576]{0,1:T(8,128)(2,1)S(1)}, u32[]{:S(2)}, u32[]{:S(2)}) %collective-permute-start.3) | collective-permute-done | bytes 294944 | tf_op jit(solution)/shard_map/ppermute | solution.py:25
  56.5 0.7 bitcast_dynamic-update-slice_fusion.3
  58.0 0.7 bitcast_dynamic-update-slice_fusion.1
  58.7 0.8 bitcast_dynamic-update-slice_fusion
  59.5 2.4 %gather_fusion = bf16[8,256,576]{1,2,0:T(8,128)(2,1)S(1)} fusion(bf16[8,256,576]{1,2,0:T(8,128)(2,1)} %bitcast_dynamic-update-slice_fusion, s32[1024]{0:T(1024)S(1)} %pad_clamp_fusion), kind=kCustom, calls=%fused_computation | custom fusion | bytes 4718624 | tf_op jit(solution)/shard_map/gather | solution.py:30
  61.8 2.6 %copy.9 = bf16[8,256,576]{2,1,0:T(8,128)(2,1)} copy(bf16[8,256,576]{1,2,0:T(8,128)(2,1)S(1)} %gather_fusion) | data formatting | bytes 4718592 | tf_op jit(solution)/shard_map/gather | solution.py:30
  64.4 2.4 %convolution_convert_fusion.1 = bf16[2048,128]{1,0:T(8,128)(2,1)S(1)} fusion(bf16[512,128]{1,0:T(8,128)(2,1)S(1)} %copy-done, bf16[2048,576]{1,0:T(8,128)(2,1)} %bitcast.84), kind=kOutput, calls=%fused_computation.195 | convolution fusion | flops 268697600 | bytes 2752512 | tf_op jit(solution)/shard_map/dot_general | solution.py:45
  66.9 1.3 collective-permute-start.8
  68.2 1.5 convolution_convert_fusion
  69.7 2.1 %collective-permute-start.10 = (bf16[1,2048,128]{2,1,0:T(8,128)(2,1)}, bf16[1,2048,128]{2,1,0:T(8,128)(2,1)}, u32[]{:S(2)}, u32[]{:S(2)}) collective-permute-start(bf16[1,2048,128]{2,1,0:T(8,128)(2,1)} %bitcast.19), channel_id=1, source_target_pairs={{0,8},{1,9},{2,10},{3,11},{4,12},{5,13},{6,14},{7,15},{16,24},{17,... | collective-permute-start | bytes 1572872 | tf_op jit(solution)/shard_map/ppermute | solution.py:37
  71.9 1.3 collective-permute-start.9
  73.2 18.9 %all-gather = s32[8,1,256]{2,1,0:T(1,128)S(1)} all-gather(s32[1,1,256]{2,1,0:T(1,128)S(1)} %bitcast.89), channel_id=1, replica_groups=mesh['grp'=2,'ctx'=2,'tp'=8] {'tp'}, dimensions={0}, use_global_device_ids=true | all-gather | bytes 9216 | tf_op jit(solution)/shard_map/all_gather | solution.py:130
  92.1 1.5 collective-permute-start.7
  93.7 1.4 copy.8
  95.2 86.1 %while.17 = (s32[]{:T(128)}, bf16[4,512,128]{2,1,0:T(8,128)(2,1)}, s32[2048]{0:T(1024)S(1)}, s32[4,512]{1,0:T(4,128)S(1)}, s32[2048]{0:T(1024)S(1)}, /*index=5*/...) while((s32[]{:T(128)}, bf16[4,512,128]{2,1,0:T(8,128)(2,1)}, ...), condition=%wide.region_17.18_spmd, body=%wide.region_0.17_spmd.sunk | while | flops 1383147008 | bytes 51794588 | solution.py:113
  101.2 1.5 fusion.289
  102.7 1.5 fusion.288
  104.3 1.5 fusion.290
  105.8 1.5 fusion.291
  107.3 1.5 fusion.292
  108.7 1.5 fusion.293
  110.2 1.5 fusion.294
  111.6 1.5 fusion.295
  113.1 1.5 fusion.296
  114.6 2.1 %fusion.297 = bf16[4,512,128]{2,1,0:T(8,128)(2,1)} fusion(bf16[4,512,128]{2,1,0:T(8,128)(2,1)} %get-tuple-element.453, s32[]{:T(128)} %get-tuple-element.452, f32[512,128]{1,0:T(8,128)S(1)} %fusion.296, f32[512,512]{0,1:T(8,128)S(1)} %get-tuple-element.411, f32[512]{0:T(512)S(1)} %get-tuple-element.412, s32[512]{0:T(512)S(1)} %bitcast.64, ...), kind=kOutput, calls=%fused_computation.43.clone.1 | convolution fusion | flops 68878336 | bytes 1585664 | tf_op jit(solution)/shard_map/while/body/eval_jaxpr/while/body/eval_jaxpr/dot_general | solution.py:105
  122.7 1.5 fusion.289
  124.3 1.5 fusion.288
  125.8 1.5 fusion.290
  127.3 1.5 fusion.291
  128.8 1.5 fusion.292
  130.2 1.5 fusion.293
  131.7 1.5 fusion.294
  133.2 1.5 fusion.295
  134.6 1.5 fusion.296
  136.1 2.1 %fusion.297 = bf16[4,512,128]{2,1,0:T(8,128)(2,1)} fusion(bf16[4,512,128]{2,1,0:T(8,128)(2,1)} %get-tuple-element.453, s32[]{:T(128)} %get-tuple-element.452, f32[512,128]{1,0:T(8,128)S(1)} %fusion.296, f32[512,512]{0,1:T(8,128)S(1)} %get-tuple-element.411, f32[512]{0:T(512)S(1)} %get-tuple-element.412, s32[512]{0:T(512)S(1)} %bitcast.64, ...), kind=kOutput, calls=%fused_computation.43.clone.1 | convolution fusion | flops 68878336 | bytes 1585664 | tf_op jit(solution)/shard_map/while/body/eval_jaxpr/while/body/eval_jaxpr/dot_general | solution.py:105
  144.2 1.5 fusion.289
  145.8 1.5 fusion.288
  147.3 1.5 fusion.290
  148.8 1.5 fusion.291
  150.3 1.5 fusion.292
  151.7 1.5 fusion.293
  153.2 1.5 fusion.294
  154.7 1.5 fusion.295
  156.1 1.5 fusion.296
  157.6 2.1 %fusion.297 = bf16[4,512,128]{2,1,0:T(8,128)(2,1)} fusion(bf16[4,512,128]{2,1,0:T(8,128)(2,1)} %get-tuple-element.453, s32[]{:T(128)} %get-tuple-element.452, f32[512,128]{1,0:T(8,128)S(1)} %fusion.296, f32[512,512]{0,1:T(8,128)S(1)} %get-tuple-element.411, f32[512]{0:T(512)S(1)} %get-tuple-element.412, s32[512]{0:T(512)S(1)} %bitcast.64, ...), kind=kOutput, calls=%fused_computation.43.clone.1 | convolution fusion | flops 68878336 | bytes 1585664 | tf_op jit(solution)/shard_map/while/body/eval_jaxpr/while/body/eval_jaxpr/dot_general | solution.py:105
  165.8 1.5 fusion.289
  167.3 1.5 fusion.288
  168.9 1.5 fusion.290
  170.3 1.5 fusion.291
  171.8 1.5 fusion.292
  173.3 1.5 fusion.293
  174.7 1.5 fusion.294
  176.2 1.5 fusion.295
  177.7 1.5 fusion.296
  179.1 2.1 %fusion.297 = bf16[4,512,128]{2,1,0:T(8,128)(2,1)} fusion(bf16[4,512,128]{2,1,0:T(8,128)(2,1)} %get-tuple-element.453, s32[]{:T(128)} %get-tuple-element.452, f32[512,128]{1,0:T(8,128)S(1)} %fusion.296, f32[512,512]{0,1:T(8,128)S(1)} %get-tuple-element.411, f32[512]{0:T(512)S(1)} %get-tuple-element.412, s32[512]{0:T(512)S(1)} %bitcast.64, ...), kind=kOutput, calls=%fused_computation.43.clone.1 | convolution fusion | flops 68878336 | bytes 1585664 | tf_op jit(solution)/shard_map/while/body/eval_jaxpr/while/body/eval_jaxpr/dot_general | solution.py:105
  (119 shorter events, 27.6 us)
Async XLA Ops:
  0.0 64.4 %copy-start = (bf16[512,128]{1,0:T(8,128)(2,1)S(1)}, bf16[512,128]{1,0:T(8,128)(2,1)}, u32[]{:S(2)}) copy-start(bf16[512,128]{1,0:T(8,128)(2,1)} %param.10) | copy-start | bytes 393220
  0.0 56.5 %copy-start.2 = (bf16[256,576]{0,1:T(8,128)(2,1)S(1)}, bf16[256,576]{0,1:T(8,128)(2,1)}, u32[]{:S(2)}) copy-start(bf16[256,576]{0,1:T(8,128)(2,1)} %param.8) | copy-start | bytes 884740
  0.0 13.2 %collective-permute-start = (bf16[256,576]{0,1:T(8,128)(2,1)}, bf16[256,576]{0,1:T(8,128)(2,1)S(1)}, u32[]{:S(2)}, u32[]{:S(2)}) collective-permute-start(bf16[256,576]{0,1:T(8,128)(2,1)} %param.8), channel_id=1, source_target_pairs={{0,1},{1,2},{2,3},{3,4},{4,5},{5,6},{6,7},{7,0},{8,9},{9,10},{10,1... | collective-permute-start | bytes 884744 | tf_op jit(solution)/shard_map/ppermute | solution.py:25
  13.2 12.3 %collective-permute-start.1 = (bf16[256,576]{0,1:T(8,128)(2,1)S(1)}, bf16[256,576]{0,1:T(8,128)(2,1)S(1)}, u32[]{:S(2)}, u32[]{:S(2)}) collective-permute-start(bf16[256,576]{0,1:T(8,128)(2,1)S(1)} %collective-permute-done), channel_id=1, source_target_pairs={{0,1},{1,2},{2,3},{3,4},{4,5},{5,6},{6,7},{7,0},{8,9},{9,10},{10,1... | collective-permute-start | bytes 884744 | tf_op jit(solution)/shard_map/ppermute | solution.py:25
  13.2 14.8 %collective-permute-start.4 = (bf16[256,576]{0,1:T(8,128)(2,1)}, bf16[256,576]{0,1:T(8,128)(2,1)S(1)}, u32[]{:S(2)}, u32[]{:S(2)}) collective-permute-start(bf16[256,576]{0,1:T(8,128)(2,1)} %param.8), channel_id=1, source_target_pairs={{1,0},{2,1},{3,2},{4,3},{5,4},{6,5},{7,6},{0,7},{9,8},{10,9},{11,1... | collective-permute-start | bytes 884744 | tf_op jit(solution)/shard_map/ppermute | solution.py:27
  25.5 13.9 %collective-permute-start.2 = (bf16[256,576]{0,1:T(8,128)(2,1)S(1)}, bf16[256,576]{0,1:T(8,128)(2,1)S(1)}, u32[]{:S(2)}, u32[]{:S(2)}) collective-permute-start(bf16[256,576]{0,1:T(8,128)(2,1)S(1)} %collective-permute-done.1), channel_id=1, source_target_pairs={{0,1},{1,2},{2,3},{3,4},{4,5},{5,6},{6,7},{7,0},{8,9},{9,10},{10,1... | collective-permute-start | bytes 884744 | tf_op jit(solution)/shard_map/ppermute | solution.py:25
  28.0 13.9 %collective-permute-start.5 = (bf16[256,576]{0,1:T(8,128)(2,1)S(1)}, bf16[256,576]{0,1:T(8,128)(2,1)S(1)}, u32[]{:S(2)}, u32[]{:S(2)}) collective-permute-start(bf16[256,576]{0,1:T(8,128)(2,1)S(1)} %collective-permute-done.4), channel_id=1, source_target_pairs={{1,0},{2,1},{3,2},{4,3},{5,4},{6,5},{7,6},{0,7},{9,8},{10,9},{11,1... | collective-permute-start | bytes 884744 | tf_op jit(solution)/shard_map/ppermute | solution.py:27
  39.4 14.2 %collective-permute-start.3 = (bf16[256,576]{0,1:T(8,128)(2,1)S(1)}, bf16[256,576]{0,1:T(8,128)(2,1)S(1)}, u32[]{:S(2)}, u32[]{:S(2)}) collective-permute-start(bf16[256,576]{0,1:T(8,128)(2,1)S(1)} %collective-permute-done.2), channel_id=1, source_target_pairs={{0,1},{1,2},{2,3},{3,4},{4,5},{5,6},{6,7},{7,0},{8,9},{9,10},{10,1... | collective-permute-start | bytes 884744 | tf_op jit(solution)/shard_map/ppermute | solution.py:25
  42.0 16.8 %collective-permute-start.6 = (bf16[256,576]{0,1:T(8,128)(2,1)S(1)}, bf16[256,576]{0,1:T(8,128)(2,1)S(1)}, u32[]{:S(2)}, u32[]{:S(2)}) collective-permute-start(bf16[256,576]{0,1:T(8,128)(2,1)S(1)} %collective-permute-done.5), channel_id=1, source_target_pairs={{1,0},{2,1},{3,2},{4,3},{5,4},{6,5},{7,6},{0,7},{9,8},{10,9},{11,1... | collective-permute-start | bytes 884744 | tf_op jit(solution)/shard_map/ppermute | solution.py:27
  64.4 3.8 %copy-start.1 = (bf16[8,256,576]{2,1,0:T(8,128)(2,1)S(1)}, bf16[8,256,576]{2,1,0:T(8,128)(2,1)}, u32[]{:S(2)}) copy-start(bf16[8,256,576]{2,1,0:T(8,128)(2,1)} %copy.9) | copy-start | bytes 7077892
  64.4 3.8 %copy-start.4 = (bf16[512,128]{1,0:T(8,128)(2,1)S(1)}, bf16[512,128]{1,0:T(8,128)(2,1)}, u32[]{:S(2)}) copy-start(bf16[512,128]{1,0:T(8,128)(2,1)} %param.11) | copy-start | bytes 393220
  66.9 6.3 %copy-start.3 = (s32[256]{0:T(256)S(1)}, s32[256]{0:T(256)}, u32[]{:S(2)}) copy-start(s32[256]{0:T(256)} %param.9) | copy-start | bytes 3076
  66.9 28.3 %collective-permute-start.8 = (bf16[1,2048,128]{2,1,0:T(8,128)(2,1)S(1)}, bf16[1,2048,128]{2,1,0:T(8,128)(2,1)S(1)}, u32[]{:S(2)}, u32[]{:S(2)}) collective-permute-start(bf16[1,2048,128]{2,1,0:T(8,128)(2,1)S(1)} %bitcast.45), channel_id=1, source_target_pairs={{0,8},{1,9},{2,10},{3,11},{4,12},{5,13},{6,14},{7,15},{16,24},{17,... | collective-permute-start | bytes 1572872 | tf_op jit(solution)/shard_map/ppermute | solution.py:37
  69.7 25.4 %collective-permute-start.10 = (bf16[1,2048,128]{2,1,0:T(8,128)(2,1)}, bf16[1,2048,128]{2,1,0:T(8,128)(2,1)}, u32[]{:S(2)}, u32[]{:S(2)}) collective-permute-start(bf16[1,2048,128]{2,1,0:T(8,128)(2,1)} %bitcast.19), channel_id=1, source_target_pairs={{0,8},{1,9},{2,10},{3,11},{4,12},{5,13},{6,14},{7,15},{16,24},{17,... | collective-permute-start | bytes 1572872 | tf_op jit(solution)/shard_map/ppermute | solution.py:37
  71.9 23.3 %collective-permute-start.9 = (bf16[2048,64]{1,0:T(8,128)(2,1)S(1)}, bf16[2048,64]{1,0:T(8,128)(2,1)S(1)}, u32[]{:S(2)}, u32[]{:S(2)}) collective-permute-start(bf16[2048,64]{1,0:T(8,128)(2,1)S(1)} %slice.153), channel_id=1, source_target_pairs={{0,8},{1,9},{2,10},{3,11},{4,12},{5,13},{6,14},{7,15},{16,24},{17,... | collective-permute-start | bytes 786440 | tf_op jit(solution)/shard_map/ppermute | solution.py:37
  92.1 3.0 %collective-permute-start.7 = (s32[2048]{0:T(1024)S(1)}, s32[2048]{0:T(1024)S(1)}, u32[]{:S(2)}, u32[]{:S(2)}) collective-permute-start(s32[2048]{0:T(1024)S(1)} %bitcast.87), channel_id=1, source_target_pairs={{0,8},{1,9},{2,10},{3,11},{4,12},{5,13},{6,14},{7,15},{16,24},{17,... | collective-permute-start | bytes 24584 | tf_op jit(solution)/shard_map/ppermute | solution.py:37
